TPU v7x, 256 devices: a whole 4x4x8 slice. The times are simulated.
256 devices in a mesh: group: 8 (over y, core), expert: 32 (over z, x).
Axes of the slice: x: 4, y: 4, z: 8, core: 2. Of those that a mesh axis runs over, the one named last changes fastest.
Arguments:
- context: bfloat16 [32768, 1024], P(('group', 'expert')), may hold values from -6 to 6
- residual: bfloat16 [32768, 2048], P(('group', 'expert')), may hold values from -0.8984375 to 0.8984375
- attn_out_w: bfloat16 [1024, 2048], P('group'), may hold values from -0.02734375 to 0.02734375
- norm_gain: float32 [2048], replicated, may hold values from 0.25 to 1.75
- router_w: bfloat16 [2048, 32], replicated, may hold values from -0.047851562 to 0.047851562
- shared_in: bfloat16 [2048, 2816], P('group'), may hold values from -0.125 to 0.125
- shared_out: bfloat16 [1408, 2048], P(None, 'group'), may hold values from -0.0234375 to 0.0234375
- expert_in: bfloat16 [32, 2048, 1536], P('expert'), may hold values from -0.125 to 0.125
- expert_out_w: bfloat16 [32, 768, 2048], P('expert'), may hold values from -0.21875 to 0.21875
- routes: int32 [32768, 6], P(('group', 'expert')), may hold values from 0 to 31, all different within a row; in each aligned block of 128 rows (0 to 127, 128 to 255, ...) at most 32 rows name the same one
Outputs:
- layer_out: bfloat16 [32768, 2048], P(('group', 'expert'))
Inputs may be any that keep to these rules, and one draw needn't show every extreme that they name: `routes`: the 6 experts of a token differ. Among the rows of one device, no expert is named by more than 32 rows, a bound that some block reaches.
All inputs are finite; a program needn't handle non-finite values.
Results may differ from a plain program's by a relative error of at most 0.022.
Values may be sent and summed in bfloat16 or wider, within the bound.
No kernel may reach another device: no remote copies, remote signals or barrier semaphores. Data moves between devices by JAX's collectives and lax.ppermute only.
A program may use at most 128 MiB of HBM per device.

v0:
```python
import jax
import jax.numpy as jnp
from jax import lax
from jax.sharding import PartitionSpec as P


def swiglu_rows(rows, w_in, w_out):
    width = w_out.shape[0]
    mid = jnp.dot(rows, w_in, preferred_element_type=jnp.float32)
    act = (jax.nn.silu(mid[:, :width]) * mid[:, width:]).astype(jnp.bfloat16)
    return jnp.dot(act, w_out, preferred_element_type=jnp.float32)


def per_device(
    context,
    residual,
    attn_out_w,
    norm_gain,
    router_w,
    shared_in,
    shared_out,
    expert_in,
    expert_out_w,
    routes,
):
    tok_rows = residual.shape[0]
    width = residual.shape[1]
    picks = routes.shape[1]
    experts = lax.axis_size("expert")
    capacity = 4 * tok_rows * picks // (3 * experts)
    columns = context
    attn = jnp.dot(
        columns,
        lax.all_gather(attn_out_w, "group", axis=0, tiled=True),
        preferred_element_type=jnp.float32,
    )
    hidden_state = (residual.astype(jnp.float32) + attn).astype(jnp.bfloat16)
    hidden_f = hidden_state.astype(jnp.float32)
    scale = lax.rsqrt(jnp.mean(hidden_f * hidden_f, axis=-1, keepdims=True) + 1e-06)
    normed = (hidden_f * scale * norm_gain).astype(jnp.bfloat16)
    logits = jnp.dot(normed, router_w, preferred_element_type=jnp.float32)
    chosen = routes[:, :, None] == jnp.arange(experts, dtype=jnp.int32)[None, None, :]
    picked = jnp.sum(jnp.where(chosen, logits[:, None, :], 0.0), axis=-1)
    sig = jax.nn.sigmoid(picked)
    gates = sig / jnp.sum(sig, axis=1, keepdims=True)
    flat_e = routes.reshape(-1)
    onehot = (flat_e[:, None] == jnp.arange(experts, dtype=jnp.int32)[None, :]).astype(jnp.int32)
    rank = jnp.cumsum(onehot, axis=0) - onehot
    position = jnp.sum(rank * onehot, axis=1)
    slot_of = flat_e * capacity + position
    token_of = jnp.arange(tok_rows * picks, dtype=jnp.int32) // picks
    source = jnp.zeros((experts * capacity,), jnp.int32).at[slot_of].set(token_of)
    filled = jnp.zeros((experts * capacity,), jnp.int32).at[slot_of].set(1)
    outgoing = jnp.where(filled[:, None] > 0, normed[source], jnp.zeros((), jnp.bfloat16))
    outgoing = outgoing.reshape(experts, capacity, width)
    local_in = expert_in[0]
    local_out = expert_out_w[0]
    arrived = lax.all_to_all(outgoing, "expert", split_axis=0, concat_axis=0, tiled=True)
    flat_rows = arrived.reshape(-1, width)
    returned = lax.all_to_all(
        swiglu_rows(flat_rows, local_in, local_out).astype(jnp.bfloat16).reshape(arrived.shape),
        "expert",
        split_axis=0,
        concat_axis=0,
        tiled=True,
    )
    gathered = returned.reshape(experts * capacity, width)[slot_of]
    weighted = gates.reshape(-1, 1) * gathered.astype(jnp.float32)
    routed = jnp.sum(weighted.reshape(tok_rows, picks, width), axis=1)
    shared_hidden = shared_out.shape[0]
    columns = normed
    shared_mid = jnp.dot(
        columns,
        lax.all_gather(shared_in, "group", axis=0, tiled=True),
        preferred_element_type=jnp.float32,
    )
    shared_act = (
        jax.nn.silu(shared_mid[:, :shared_hidden]) * shared_mid[:, shared_hidden:]
    ).astype(jnp.bfloat16)
    shared_y = jnp.dot(
        shared_act,
        lax.all_gather(shared_out, "group", axis=1, tiled=True),
        preferred_element_type=jnp.float32,
    )
    return (hidden_f + shared_y + routed).astype(jnp.bfloat16)


def solution(mesh):
    placed = (
        P(("group", "expert"), None),
        P(("group", "expert"), None),
        P("group", None),
        P(),
        P(),
        P("group", None),
        P(None, "group"),
        P("expert", None, None),
        P("expert", None, None),
        P(("group", "expert"), None),
    )
    return jax.shard_map(
        per_device,
        mesh=mesh,
        in_specs=placed,
        out_specs=P(("group", "expert"), None),
        check_vma=False,
    )
```

profile of v0, /device:TPU:2, one launch (start us, length us, event | category | flops | bytes accessed | tf_op | source)
XLA Modules:
  0.0 323.8 jit_solution(1857204493511975896)
XLA Ops:
  6.5 0.7 all-gather.4.cloned.1.call-update
  7.3 0.7 all-gather.6.cloned.1.call-update
  8.0 0.8 copy.21
  8.8 0.1 eq.45
  9.0 0.1 eq.41
  9.1 1.7 reduce-window.6
  10.9 0.3 slice_reduce_fusion
  11.1 0.7 broadcast_multiply_fusion
  11.8 0.1 copy.20
  12.0 0.1 mul.71
  12.2 3.4 %scatter_custom_fusion.1 = s32[1024]{0:T(1024)S(1)} fusion(s32[768]{0:T(1024)S(1)} %fusion.21, s32[768]{0:T(1024)S(1)} %add_select_fusion, s32[]{:T(128)} %constant.16.clone.1), kind=kCustom, calls=%fused_computation.51 | custom fusion | bytes 4100 | tf_op jit(solution)/shard_map/scatter | solution.py:52
  15.6 3.4 %scatter_custom_fusion = s32[1024]{0:T(1024)S(1)} fusion(s32[768]{0:T(1024)S(1)} %fusion.21, s32[768]{0:T(1024)S(1)} %broadcast.97, s32[]{:T(128)} %constant.16.clone.1), kind=kCustom, calls=%fused_computation.54 | custom fusion | bytes 4100 | tf_op jit(solution)/shard_map/scatter | solution.py:53
  19.1 27.8 %all-gather.4.cloned.1.call-done = bf16[1024,2048]{1,0:T(8,128)(2,1)} async-done(((bf16[128,2048]{1,0:T(8,128)(2,1)}), bf16[1024,2048]{1,0:T(8,128)(2,1)}) %all-gather.4.cloned.1.call-update) | async-done | bytes 4194320 | tf_op jit(solution)/shard_map/all_gather | solution.py:34
  46.9 3.2 multiply_reduce_fusion.1
  50.1 0.9 copy-done.3
  51.1 1.0 multiply_convert_fusion
  52.0 9.9 %gather_fusion = bf16[1024,2048]{1,0:T(8,128)(2,1)} fusion(bf16[128,2048]{1,0:T(8,128)(2,1)} %multiply_convert_fusion, s32[1024]{0:T(1024)S(1)} %fusion.19), kind=kCustom, calls=%fused_computation | custom fusion | bytes 8392704 | tf_op jit(solution)/shard_map/gather | solution.py:54
  62.0 5.2 %broadcast_select_fusion = bf16[32,32,2048]{2,1,0:T(8,128)(2,1)} fusion(bf16[32,32,2048]{2,1,0:T(8,128)(2,1)} %bitcast.38, pred[32,32]{1,0:T(8,128)(4,1)S(1)} %broadcast_in_dim.46), kind=kLoop, calls=%fused_computation.7 | loop fusion | flops 2097152 | bytes 8389632 | tf_op jit(solution)/shard_map/jit(_where)/select_n | solution.py:54
  67.2 10.2 %all-to-all-start = ((bf16[32,32,2048]{2,1,0:T(8,128)(2,1)}), bf16[32,32,2048]{2,1,0:T(8,128)(2,1)}, u32[]{:S(2)}, u32[]{:S(2)}) async-start(bf16[32,32,2048]{2,1,0:T(8,128)(2,1)} %broadcast_select_fusion), calls=%async_computation | async-start | bytes 8388608 | tf_op jit(solution)/shard_map/all_to_all | solution.py:58
  77.4 0.7 all-gather.8.cloned.1.call-update
  78.1 97.0 %all-to-all-done = bf16[32,32,2048]{2,1,0:T(8,128)(2,1)} async-done(((bf16[32,32,2048]{2,1,0:T(8,128)(2,1)}), bf16[32,32,2048]{2,1,0:T(8,128)(2,1)}, u32[]{:S(2)}, u32[]{:S(2)}) %all-to-all-start) | async-done | bytes 4194336 | tf_op jit(solution)/shard_map/all_to_all | solution.py:58
  175.1 10.0 %fusion = f32[1024,1536]{1,0:T(8,128)S(1)} fusion(bf16[1024,2048]{1,0:T(8,128)(2,1)} %bitcast.2, bf16[1,2048,1536]{2,1,0:T(8,128)(2,1)} %param.17), kind=kOutput, calls=%fused_computation.5 | convolution fusion | flops 6442450944 | bytes 16777216 | tf_op jit(solution)/shard_map/dot_general | solution.py:9
  185.2 5.1 %convolution_convert_fusion = bf16[1024,2048]{1,0:T(8,128)(2,1)} fusion(bf16[1,768,2048]{2,1,0:T(8,128)(2,1)S(1)} %copy-done, f32[1024,1536]{1,0:T(8,128)S(1)} %fusion), kind=kOutput, calls=%fused_computation.8 | convolution fusion | flops 3228041216 | bytes 13631488 | tf_op jit(solution)/shard_map/dot_general | solution.py:11
  190.3 5.0 %all-to-all-start.1 = ((bf16[32,32,2048]{2,1,0:T(8,128)(2,1)}), bf16[32,32,2048]{2,1,0:T(8,128)(2,1)}, u32[]{:S(2)}, u32[]{:S(2)}) async-start(bf16[32,32,2048]{2,1,0:T(8,128)(2,1)} %bitcast.39), calls=%async_computation.1 | async-start | bytes 8388608 | tf_op jit(solution)/shard_map/all_to_all | solution.py:60
  195.3 0.3 fusion.29
  195.6 0.1 copy.19
  195.8 7.1 %fusion.28 = f32[128,2816]{1,0:T(8,128)} fusion(bf16[128,2048]{1,0:T(8,128)(2,1)S(1)} %copy-done.2, bf16[2048,2816]{1,0:T(8,128)(2,1)} %all-gather.6.cloned.1.call-done), kind=kOutput, calls=%fused_computation.59 | convolution fusion | flops 1476395008 | bytes 13500416 | tf_op jit(solution)/shard_map/dot_general | solution.py:72
  202.9 88.4 %all-to-all-done.1 = bf16[32,32,2048]{2,1,0:T(8,128)(2,1)} async-done(((bf16[32,32,2048]{2,1,0:T(8,128)(2,1)}), bf16[32,32,2048]{2,1,0:T(8,128)(2,1)}, u32[]{:S(2)}, u32[]{:S(2)}) %all-to-all-start.1) | async-done | bytes 4194336 | tf_op jit(solution)/shard_map/all_to_all | solution.py:60
  291.3 9.1 %gather_fusion.1 = bf16[768,2048]{1,0:T(8,128)(2,1)S(1)} fusion(bf16[1024,2048]{1,0:T(8,128)(2,1)} %bitcast.6, s32[1024]{0:T(1024)S(1)} %pad_clamp_fusion), kind=kCustom, calls=%fused_computation.1 | custom fusion | bytes 6294528 | tf_op jit(solution)/shard_map/gather | solution.py:67
  300.3 3.7 %reshape.103 = f32[128,6,2048]{2,1,0:T(8,128)} reshape(bf16[768,2048]{1,0:T(8,128)(2,1)S(1)} %gather_fusion.1) | data formatting | bytes 9437184 | tf_op jit(solution)/shard_map/convert_element_type | solution.py:68
  304.0 7.8 %multiply_reduce_fusion = f32[128,2048]{1,0:T(8,128)} fusion(f32[128,6,2048]{2,1,0:T(8,128)} %reshape.103, f32[128,6]{1,0:T(8,128)S(1)} %copy.19), kind=kLoop, calls=%fused_computation.4 | loop fusion | flops 2883584 | bytes 7343104 | tf_op jit(solution)/shard_map/reduce_sum | solution.py:69
  311.8 5.5 %fusion.5 = bf16[128,2048]{1,0:T(8,128)(2,1)} fusion(f32[128,2048]{1,0:T(8,128)} %multiply_reduce_fusion, f32[128,2048]{1,0:T(8,128)} %copy-done.3, bf16[1408,2048]{1,0:T(8,128)(2,1)} %all-gather.8.cloned.1.call-done, f32[128,2816]{1,0:T(8,128)} %fusion.28), kind=kOutput, calls=%fused_computation.15 | convolution fusion | flops 740065280 | bytes 9830400 | tf_op jit(solution)/shard_map/dot_general | solution.py:80
  (32 shorter events, 0.5 us)
Async XLA Ops:
  6.5 178.6 %copy-start = (bf16[1,768,2048]{2,1,0:T(8,128)(2,1)S(1)}, bf16[1,768,2048]{2,1,0:T(8,128)(2,1)}, u32[]{:S(2)}) copy-start(bf16[1,768,2048]{2,1,0:T(8,128)(2,1)} %param.18) | copy-start | bytes 9437188
  6.5 40.4 %all-gather.4.cloned.1.call-start = ((), (), s32[]{:S(2)}) async-start(), calls=%async_computation.2 | async-start | bytes 4718592 | tf_op jit(solution)/shard_map/all_gather | solution.py:34
  7.3 43.8 %copy-start.6 = (f32[2048]{0:T(1024)S(1)}, f32[2048]{0:T(1024)}, u32[]{:S(2)}) copy-start(f32[2048]{0:T(1024)} %param.13) | copy-start | bytes 24580
  7.3 188.5 %all-gather.6.cloned.1.call-start = ((), (), s32[]{:S(2)}) async-start(), calls=%async_computation.3 | async-start | bytes 12976128 | tf_op jit(solution)/shard_map/all_gather | solution.py:74
  50.1 1.0 copy-start.3
  67.2 108.0 %all-to-all-start = ((bf16[32,32,2048]{2,1,0:T(8,128)(2,1)}), bf16[32,32,2048]{2,1,0:T(8,128)(2,1)}, u32[]{:S(2)}, u32[]{:S(2)}) async-start(bf16[32,32,2048]{2,1,0:T(8,128)(2,1)} %broadcast_select_fusion), calls=%async_computation | async-start | bytes 8388608 | tf_op jit(solution)/shard_map/all_to_all | solution.py:58
  77.4 234.4 %all-gather.8.cloned.1.call-start = ((), (), s32[]{:S(2)}) async-start(), calls=%async_computation.4 | async-start | bytes 6488064 | tf_op jit(solution)/shard_map/all_gather | solution.py:82
  190.3 5.0 %copy-start.2 = (bf16[128,2048]{1,0:T(8,128)(2,1)S(1)}, bf16[128,2048]{1,0:T(8,128)(2,1)}, u32[]{:S(2)}) copy-start(bf16[128,2048]{1,0:T(8,128)(2,1)} %multiply_convert_fusion) | copy-start | bytes 1572868
  190.3 5.0 %copy-start.4 = (bf16[2048,32]{0,1:T(8,128)(2,1)S(1)}, bf16[2048,32]{0,1:T(8,128)(2,1)}, u32[]{:S(2)}) copy-start(bf16[2048,32]{0,1:T(8,128)(2,1)} %param.14) | copy-start | bytes 393220
  190.3 5.3 %copy-start.5 = (s32[128,6]{0,1:T(8,128)S(1)}, s32[128,6]{0,1:T(8,128)}, u32[]{:S(2)}) copy-start(s32[128,6]{0,1:T(8,128)} %param.19) | copy-start | bytes 9220
  190.3 101.0 %all-to-all-start.1 = ((bf16[32,32,2048]{2,1,0:T(8,128)(2,1)}), bf16[32,32,2048]{2,1,0:T(8,128)(2,1)}, u32[]{:S(2)}, u32[]{:S(2)}) async-start(bf16[32,32,2048]{2,1,0:T(8,128)(2,1)} %bitcast.39), calls=%async_computation.1 | async-start | bytes 8388608 | tf_op jit(solution)/shard_map/all_to_all | solution.py:60
  304.0 13.3 %copy-start.1 = (bf16[1,768,2048]{2,1,0:T(8,128)(2,1)S(1)}, bf16[1,768,2048]{2,1,0:T(8,128)(2,1)}, u32[]{:S(2)}) copy-start(bf16[1,768,2048]{2,1,0:T(8,128)(2,1)} %param.18) | copy-start | bytes 9437188
Sparse Core Ops, SparseCore 0:
  9.2 37.6 all-gather.3
  48.7 65.4 all-gather.5
  116.1 45.6 all-gather.7
where the time goes:
time: 324 us
  waiting for transfers between devices  215 us (66%)
  local copies, waits for them, and re-layouts  32.2 us (10%)
  matrix products  31.2 us (10%)
  other arithmetic  16.6 us (5%)
  starting transfers between devices  15.2 us (5%)
  between operations  13.3 us (4%)
    all_to_all x1, waiting for transfers between devices, per_device(): lax.all_to_all(outgoing, 'expert', split_axis=0, concat_axis=0, tiled=True)  97 us
    all_to_all x1, waiting for transfers between devices, per_device(): lax.all_to_all(swiglu_rows(flat_rows, local_in, local_out).astype(jnp.bfl...  88.4 us
    all_gather x1, waiting for transfers between devices, per_device(): lax.all_gather(attn_out_w, 'group', axis=0, tiled=True)  27.8 us
    all_to_all x1, starting transfers between devices, per_device(): lax.all_to_all(outgoing, 'expert', split_axis=0, concat_axis=0, tiled=True)  10.2 us
    dot_general x1, matrix products, swiglu_rows(): mid = jnp.dot(rows, w_in, preferred_element_type=jnp.float32)  10 us
    gather x1, local copies, waits for them, and re-layouts, per_device(): normed[source]  9.94 us
    gather x1, local copies, waits for them, and re-layouts, per_device(): gathered = returned.reshape(experts * capacity, width)[slot_of]  9.06 us
    reduce_sum x1, other arithmetic, per_device(): routed = jnp.sum(weighted.reshape(tok_rows, picks, width), axis=1)  7.77 us
  transfers between devices with their start and end apart: 5, of which 3 were waited for; matrix products, arithmetic and copies ran while one was open for 23% of the time, Pallas kernels for 0%

commit v1 on v0

--- a/solution.py
+++ b/solution.py
@@ -31,7 +31,9 @@
     columns = context
     attn = jnp.dot(
         columns,
-        lax.all_gather(attn_out_w, "group", axis=0, tiled=True),
+        jnp.concatenate(
+            lax.all_to_all(jnp.stack([attn_out_w] * lax.axis_size("group")), "group", 0, 0), axis=0
+        ),
         preferred_element_type=jnp.float32,
     )
     hidden_state = (residual.astype(jnp.float32) + attn).astype(jnp.bfloat16)

time: 324 us -> 384 us (1.19)
  waiting for transfers between devices: 215 us -> 261 us
  starting transfers between devices: 15.2 us -> 26 us
    all_to_all x0 -> x1, waiting for transfers between devices: none -> 75.9 us  [per_device(): lax.all_to_all(jnp.stack([attn_out_w] * lax.axis_size('group')), 'group',...]
    all_gather x1 -> x0, waiting for transfers between devices: 27.8 us -> none  [per_device(): lax.all_gather(attn_out_w, 'group', axis=0, tiled=True)]
    all_to_all x1, waiting for transfers between devices: 97 us -> 91.5 us  [per_device(): lax.all_to_all(outgoing, 'expert', split_axis=0, concat_axis=0, tiled=True)]
    all_to_all x0 -> x1, starting transfers between devices: none -> 4.68 us  [per_device(): lax.all_to_all(jnp.stack([attn_out_w] * lax.axis_size('group')), 'group',...]
  transfers between devices with their start and end apart: 5 -> 5, of which waited for: 3 -> 3; matrix products, arithmetic and copies ran while one was open for 23% -> 20% of each run, Pallas kernels for 0% -> 0%
where the time goes in v1:
time: 384 us; the launch traced here: 382 us
  waiting for transfers between devices  261 us (68%)
  local copies, waits for them, and re-layouts  35.5 us (9%)
  matrix products  31.4 us (8%)
  starting transfers between devices  26 us (7%)
  other arithmetic  15.1 us (4%)
  between operations  13.6 us (4%)
    all_to_all x1, waiting for transfers between devices, per_device(): lax.all_to_all(swiglu_rows(flat_rows, local_in, local_out).astype(jnp.bfl...  91.8 us
    all_to_all x1, waiting for transfers between devices, per_device(): lax.all_to_all(outgoing, 'expert', split_axis=0, concat_axis=0, tiled=True)  91.5 us
    all_to_all x1, waiting for transfers between devices, per_device(): lax.all_to_all(jnp.stack([attn_out_w] * lax.axis_size('group')), 'group',...  75.9 us
    all_to_all x1, starting transfers between devices, per_device(): lax.all_to_all(outgoing, 'expert', split_axis=0, concat_axis=0, tiled=True)  13.3 us
    dot_general x1, matrix products, swiglu_rows(): mid = jnp.dot(rows, w_in, preferred_element_type=jnp.float32)  10 us
    gather x1, local copies, waits for them, and re-layouts, per_device(): normed[source]  9.95 us
    gather x1, local copies, waits for them, and re-layouts, per_device(): gathered = returned.reshape(experts * capacity, width)[slot_of]  9.06 us
    all_to_all x1, starting transfers between devices, per_device(): lax.all_to_all(swiglu_rows(flat_rows, local_in, local_out).astype(jnp.bfl...  8.02 us
  transfers between devices with their start and end apart: 5, of which 3 were waited for; matrix products, arithmetic and copies ran while one was open for 20% of the time, Pallas kernels for 0%

profile of v1, /device:TPU:2, one launch (start us, length us, event | category | flops | bytes accessed | tf_op | source)
XLA Modules:
  0.0 382.3 jit_solution(2747298494307702113)
XLA Ops:
  6.5 0.7 all-gather.3.cloned.1.call-update
  7.3 3.8 stack.2
  11.0 4.7 %all-to-all-start = ((bf16[8,128,2048]{2,1,0:T(8,128)(2,1)}), bf16[8,128,2048]{2,1,0:T(8,128)(2,1)}, u32[]{:S(2)}, u32[]{:S(2)}) async-start(bf16[8,128,2048]{2,1,0:T(8,128)(2,1)} %stack.2), calls=%async_computation | async-start | bytes 8388608 | tf_op jit(solution)/shard_map/all_to_all | solution.py:35
  15.7 0.1 copy.21
  15.9 0.1 eq.45
  16.0 0.1 eq.41
  16.1 1.7 reduce-window.6
  17.9 0.3 slice_reduce_fusion
  18.2 0.1 copy.20
  18.3 0.1 mul.71
  18.6 3.4 scatter_custom_fusion.1
  22.0 3.4 scatter_custom_fusion
  25.5 75.9 %all-to-all-done = bf16[8,128,2048]{2,1,0:T(8,128)(2,1)} async-done(((bf16[8,128,2048]{2,1,0:T(8,128)(2,1)}), bf16[8,128,2048]{2,1,0:T(8,128)(2,1)}, u32[]{:S(2)}, u32[]{:S(2)}) %all-to-all-start) | async-done | bytes 4194336 | tf_op jit(solution)/shard_map/all_to_all | solution.py:35
  101.4 3.2 multiply_reduce_fusion.1
  104.7 1.0 copy-done.3
  105.7 1.0 multiply_convert_fusion
  106.6 9.9 %gather_fusion = bf16[1024,2048]{1,0:T(8,128)(2,1)} fusion(bf16[128,2048]{1,0:T(8,128)(2,1)} %multiply_convert_fusion, s32[1024]{0:T(1024)S(1)} %fusion.19), kind=kCustom, calls=%fused_computation | custom fusion | bytes 8392704 | tf_op jit(solution)/shard_map/gather | solution.py:56
  116.6 4.6 %broadcast_select_fusion = bf16[32,32,2048]{2,1,0:T(8,128)(2,1)} fusion(bf16[32,32,2048]{2,1,0:T(8,128)(2,1)} %bitcast.39, pred[32,32]{1,0:T(8,128)(4,1)S(1)} %broadcast_in_dim.46), kind=kLoop, calls=%fused_computation.7 | loop fusion | flops 2097152 | bytes 8389632 | tf_op jit(solution)/shard_map/jit(_where)/select_n | solution.py:56
  121.2 13.3 %all-to-all-start.1 = ((bf16[32,32,2048]{2,1,0:T(8,128)(2,1)}), bf16[32,32,2048]{2,1,0:T(8,128)(2,1)}, u32[]{:S(2)}, u32[]{:S(2)}) async-start(bf16[32,32,2048]{2,1,0:T(8,128)(2,1)} %broadcast_select_fusion), calls=%async_computation.1 | async-start | bytes 8388608 | tf_op jit(solution)/shard_map/all_to_all | solution.py:60
  134.5 0.7 all-gather.5.cloned.1.call-update
  135.2 91.5 %all-to-all-done.1 = bf16[32,32,2048]{2,1,0:T(8,128)(2,1)} async-done(((bf16[32,32,2048]{2,1,0:T(8,128)(2,1)}), bf16[32,32,2048]{2,1,0:T(8,128)(2,1)}, u32[]{:S(2)}, u32[]{:S(2)}) %all-to-all-start.1) | async-done | bytes 4194336 | tf_op jit(solution)/shard_map/all_to_all | solution.py:60
  226.7 10.0 %fusion = f32[1024,1536]{1,0:T(8,128)S(1)} fusion(bf16[1024,2048]{1,0:T(8,128)(2,1)} %bitcast.3, bf16[1,2048,1536]{2,1,0:T(8,128)(2,1)} %param.17), kind=kOutput, calls=%fused_computation.5 | convolution fusion | flops 6442450944 | bytes 16777216 | tf_op jit(solution)/shard_map/dot_general | solution.py:9
  236.7 5.1 %convolution_convert_fusion = bf16[1024,2048]{1,0:T(8,128)(2,1)} fusion(bf16[1,768,2048]{2,1,0:T(8,128)(2,1)S(1)} %copy-done, f32[1024,1536]{1,0:T(8,128)S(1)} %fusion), kind=kOutput, calls=%fused_computation.8 | convolution fusion | flops 3228041216 | bytes 13631488 | tf_op jit(solution)/shard_map/dot_general | solution.py:11
  241.8 8.0 %all-to-all-start.2 = ((bf16[32,32,2048]{2,1,0:T(8,128)(2,1)}), bf16[32,32,2048]{2,1,0:T(8,128)(2,1)}, u32[]{:S(2)}, u32[]{:S(2)}) async-start(bf16[32,32,2048]{2,1,0:T(8,128)(2,1)} %bitcast.40), calls=%async_computation.2 | async-start | bytes 8388608 | tf_op jit(solution)/shard_map/all_to_all | solution.py:62
  249.8 0.3 fusion.29
  250.2 0.1 copy.19
  250.3 91.8 %all-to-all-done.2 = bf16[32,32,2048]{2,1,0:T(8,128)(2,1)} async-done(((bf16[32,32,2048]{2,1,0:T(8,128)(2,1)}), bf16[32,32,2048]{2,1,0:T(8,128)(2,1)}, u32[]{:S(2)}, u32[]{:S(2)}) %all-to-all-start.2) | async-done | bytes 4194336 | tf_op jit(solution)/shard_map/all_to_all | solution.py:62
  342.2 9.1 %gather_fusion.1 = bf16[768,2048]{1,0:T(8,128)(2,1)S(1)} fusion(bf16[1024,2048]{1,0:T(8,128)(2,1)} %bitcast.7, s32[1024]{0:T(1024)S(1)} %pad_clamp_fusion), kind=kCustom, calls=%fused_computation.1 | custom fusion | bytes 6294528 | tf_op jit(solution)/shard_map/gather | solution.py:69
  351.2 3.8 reshape.109
  355.0 7.6 %multiply_reduce_fusion = f32[128,2048]{1,0:T(8,128)} fusion(f32[128,6,2048]{2,1,0:T(8,128)} %reshape.109, f32[128,6]{1,0:T(8,128)S(1)} %copy.19), kind=kLoop, calls=%fused_computation.4 | loop fusion | flops 2883584 | bytes 7343104 | tf_op jit(solution)/shard_map/reduce_sum | solution.py:71
  362.6 7.4 %fusion.28 = f32[128,2816]{1,0:T(8,128)} fusion(bf16[128,2048]{1,0:T(8,128)(2,1)} %multiply_convert_fusion, bf16[2048,2816]{1,0:T(8,128)(2,1)} %all-gather.3.cloned.1.call-done), kind=kOutput, calls=%fused_computation.59 | convolution fusion | flops 1476395008 | bytes 13500416 | tf_op jit(solution)/shard_map/dot_general | solution.py:74
  370.0 5.5 %fusion.5 = bf16[128,2048]{1,0:T(8,128)(2,1)} fusion(f32[128,2048]{1,0:T(8,128)} %multiply_reduce_fusion, f32[128,2048]{1,0:T(8,128)} %copy-done.3, bf16[1408,2048]{1,0:T(8,128)(2,1)} %all-gather.5.cloned.1.call-done, f32[128,2816]{1,0:T(8,128)} %fusion.28), kind=kOutput, calls=%fused_computation.15 | convolution fusion | flops 740065280 | bytes 9830400 | tf_op jit(solution)/shard_map/dot_general | solution.py:82
  (32 shorter events, 0.4 us)
Async XLA Ops:
  6.5 230.2 %copy-start = (bf16[1,768,2048]{2,1,0:T(8,128)(2,1)S(1)}, bf16[1,768,2048]{2,1,0:T(8,128)(2,1)}, u32[]{:S(2)}) copy-start(bf16[1,768,2048]{2,1,0:T(8,128)(2,1)} %param.18) | copy-start | bytes 9437188
  6.5 356.0 %all-gather.3.cloned.1.call-start = ((), (), s32[]{:S(2)}) async-start(), calls=%async_computation.3 | async-start | bytes 12976128 | tf_op jit(solution)/shard_map/all_gather | solution.py:76
  11.0 4.7 %copy-start.5 = (s32[128,6]{0,1:T(8,128)S(1)}, s32[128,6]{0,1:T(8,128)}, u32[]{:S(2)}) copy-start(s32[128,6]{0,1:T(8,128)} %param.19) | copy-start | bytes 9220
  11.0 90.4 %all-to-all-start = ((bf16[8,128,2048]{2,1,0:T(8,128)(2,1)}), bf16[8,128,2048]{2,1,0:T(8,128)(2,1)}, u32[]{:S(2)}, u32[]{:S(2)}) async-start(bf16[8,128,2048]{2,1,0:T(8,128)(2,1)} %stack.2), calls=%async_computation | async-start | bytes 8388608 | tf_op jit(solution)/shard_map/all_to_all | solution.py:35
  15.7 90.0 %copy-start.6 = (f32[2048]{0:T(1024)S(1)}, f32[2048]{0:T(1024)}, u32[]{:S(2)}) copy-start(f32[2048]{0:T(1024)} %param.13) | copy-start | bytes 24580
  104.6 1.0 copy-start.3
  121.2 105.5 %all-to-all-start.1 = ((bf16[32,32,2048]{2,1,0:T(8,128)(2,1)}), bf16[32,32,2048]{2,1,0:T(8,128)(2,1)}, u32[]{:S(2)}, u32[]{:S(2)}) async-start(bf16[32,32,2048]{2,1,0:T(8,128)(2,1)} %broadcast_select_fusion), calls=%async_computation.1 | async-start | bytes 8388608 | tf_op jit(solution)/shard_map/all_to_all | solution.py:60
  134.4 235.5 %all-gather.5.cloned.1.call-start = ((), (), s32[]{:S(2)}) async-start(), calls=%async_computation.4 | async-start | bytes 6488064 | tf_op jit(solution)/shard_map/all_gather | solution.py:84
  241.8 8.1 %copy-start.2 = (bf16[128,2048]{1,0:T(8,128)(2,1)S(1)}, bf16[128,2048]{1,0:T(8,128)(2,1)}, u32[]{:S(2)}) copy-start(bf16[128,2048]{1,0:T(8,128)(2,1)} %multiply_convert_fusion) | copy-start | bytes 1572868
  241.8 8.1 %copy-start.4 = (bf16[2048,32]{0,1:T(8,128)(2,1)S(1)}, bf16[2048,32]{0,1:T(8,128)(2,1)}, u32[]{:S(2)}) copy-start(bf16[2048,32]{0,1:T(8,128)(2,1)} %param.14) | copy-start | bytes 393220
  241.8 100.4 %all-to-all-start.2 = ((bf16[32,32,2048]{2,1,0:T(8,128)(2,1)}), bf16[32,32,2048]{2,1,0:T(8,128)(2,1)}, u32[]{:S(2)}, u32[]{:S(2)}) async-start(bf16[32,32,2048]{2,1,0:T(8,128)(2,1)} %bitcast.40), calls=%async_computation.2 | async-start | bytes 8388608 | tf_op jit(solution)/shard_map/all_to_all | solution.py:62
  362.6 12.9 %copy-start.1 = (bf16[1,768,2048]{2,1,0:T(8,128)(2,1)S(1)}, bf16[1,768,2048]{2,1,0:T(8,128)(2,1)}, u32[]{:S(2)}) copy-start(bf16[1,768,2048]{2,1,0:T(8,128)(2,1)} %param.18) | copy-start | bytes 9437188
Sparse Core Ops, SparseCore 0:
  9.2 104.0 all-gather.2
  137.1 43.7 all-gather.4
